TPU v7x, 512 devices: a whole 4x8x8 slice. The times are simulated.
512 devices in a mesh: seq: 16 (over z, core), expert: 32 (over x, y).
Axes of the slice: x: 4, y: 8, z: 8, core: 2. Of those that a mesh axis runs over, the one named last changes fastest.
Arguments:
- hidden: bfloat16 [32, 1024, 2048], P('expert', 'seq'), may hold values from -6 to 6
- queries: bfloat16 [32, 1024, 4608], P('expert', 'seq'), may hold values from -5 to 5
- suffix_latent: bfloat16 [32, 1024, 576], P('expert', 'seq'), may hold values from -6 to 6
- prefix_latent: bfloat16 [2, 1024, 576], P(None, 'seq'), may hold values from -6 to 6
- lengths: int32 [32, 4], P('expert'), may hold values from 1 to 512, 1024 in all within a row
- prefix_of: int32 [32, 4], P('expert'), may hold values from 0 to 1
- value_up: bfloat16 [8, 512, 128], replicated, may hold values from -1 to 1
- out_proj: bfloat16 [1024, 2048], P(None, 'expert'), may hold values from -0.1875 to 0.1875
- norm_gain: float32 [2048], replicated, may hold values from 0.5 to 1.5
- router: bfloat16 [2048, 32], replicated, may hold values from -0.0625 to 0.0625
- routes: int32 [32, 1024, 6], P('expert', 'seq'), may hold values from 0 to 31, all different within a row; in each aligned block of 64 rows (0 to 63, 64 to 127, ..., all dimensions but the last counted through in order) at most 16 rows name the same one
- expert_in: bfloat16 [32, 2048, 1408], P('expert', 'seq'), may hold values from -0.125 to 0.125
- expert_out: bfloat16 [32, 2048, 704], P('expert', 'seq'), may hold values from -1.25 to 1.25
Outputs:
- layer_out: bfloat16 [32, 1024, 2048], P('expert', 'seq')
Inputs may be any that keep to these rules, and one draw needn't show every extreme that they name: `routes`: among the rows of one device (aligned blocks of 64 tokens) no expert is named more than 16 times, a bound that some block reaches; a token's 6 experts differ. `lengths`: each row sums to 1024; its longest request has exactly 512 tokens.
All inputs are finite; a program needn't handle non-finite values.
Results may differ from a plain program's by a relative error of at most 0.013.
Values may be sent and summed in bfloat16 or wider, within the bound.
No kernel may reach another device: no remote copies, remote signals or barrier semaphores. Data moves between devices by JAX's collectives and lax.ppermute only.
A program may use at most 128 MiB of HBM per device.

v0:
```python
import jax
import jax.numpy as jnp
from jax import lax
from jax.sharding import PartitionSpec as P

qk_scale = 192.0 ** (-0.5)
big_negative = -1e30


def request_of(positions, request_ends):
    return jnp.sum((positions[:, None] >= request_ends[None, :]).astype(jnp.int32), axis=1)


def merge_scores(running, scores, allowed, values):
    running_max, running_sum, running_acc = running
    new_max = jnp.maximum(running_max, jnp.max(jnp.where(allowed, scores, big_negative), axis=2))
    weights = jnp.where(allowed, jnp.exp(scores - new_max[:, :, None]), 0.0)
    new_sum = jnp.sum(weights, axis=2)
    new_acc = jnp.einsum(
        "thn,nl->thl", weights.astype(jnp.bfloat16), values, preferred_element_type=jnp.float32
    )
    return (new_max, new_sum, new_acc)


def local(
    hidden,
    queries,
    suffix_latent,
    prefix_latent,
    lengths,
    prefix_of,
    value_up,
    out_proj,
    norm_gain,
    router,
    routes,
    expert_in,
    expert_out,
):
    local_tokens = hidden.shape[1]
    model_width = hidden.shape[2]
    key_width = suffix_latent.shape[2]
    head_count = value_up.shape[0]
    latent_width = value_up.shape[1]
    expert_count = router.shape[1]
    top_count = routes.shape[2]
    capacity = 4 * local_tokens * top_count // (3 * expert_count)
    request_count = lengths.shape[1]
    request_ends = jnp.cumsum(lengths[0])
    my_positions = lax.axis_index("seq") * local_tokens + jnp.arange(local_tokens, dtype=jnp.int32)
    my_requests = request_of(my_positions, request_ends)
    request_ids = jnp.arange(request_count, dtype=jnp.int32)
    chosen = jnp.sum(
        jnp.where(my_requests[:, None] == request_ids[None, :], prefix_of[0][None, :], 0), axis=1
    )
    prefix_pick = chosen[:, None] == jnp.arange(2, dtype=jnp.int32)[None, :]
    single_prefix = jnp.all(chosen == chosen[0])
    my_prefix = chosen[0]
    query_rows = queries[0].reshape(local_tokens, head_count, key_width)
    start_state = (
        jnp.full((local_tokens, head_count), big_negative, jnp.float32),
        jnp.zeros((local_tokens, head_count), jnp.float32),
        jnp.zeros((local_tokens, head_count, latent_width), jnp.float32),
    )
    suffix_piece = lax.all_gather(suffix_latent, "seq", axis=1, tiled=True)
    prefix_piece = lax.all_gather(prefix_latent, "seq", axis=1, tiled=True)
    piece_rows = suffix_piece.shape[1]
    suffix_keys = suffix_piece[0]
    key_positions = jnp.arange(piece_rows, dtype=jnp.int32)
    key_requests = request_of(key_positions, request_ends)
    suffix_allowed = (key_requests[None, :] == my_requests[:, None]) & (
        key_positions[None, :] <= my_positions[:, None]
    )
    suffix_scores = (
        jnp.einsum("thk,nk->thn", query_rows, suffix_keys, preferred_element_type=jnp.float32)
        * qk_scale
    )

    def one_prefix(running_state):
        chosen_keys = lax.dynamic_index_in_dim(prefix_piece, my_prefix, 0, keepdims=False)
        prefix_scores = (
            jnp.einsum("thk,nk->thn", query_rows, chosen_keys, preferred_element_type=jnp.float32)
            * qk_scale
        )
        scores = jnp.concatenate([suffix_scores, prefix_scores], axis=2)
        every_key = jnp.ones((local_tokens, piece_rows), dtype=bool)
        allowed = jnp.concatenate([suffix_allowed, every_key], axis=1)[:, None, :]
        values = jnp.concatenate(
            [suffix_keys[:, :latent_width], chosen_keys[:, :latent_width]], axis=0
        )
        return merge_scores(running_state, scores, allowed, values)

    def two_prefixes(running_state):
        prefix_scores = (
            jnp.einsum(
                "thk,pnk->thpn", query_rows, prefix_piece, preferred_element_type=jnp.float32
            )
            * qk_scale
        )
        scores = jnp.concatenate(
            [suffix_scores, prefix_scores.reshape(local_tokens, head_count, 2 * piece_rows)], axis=2
        )
        prefix_allowed = jnp.broadcast_to(
            prefix_pick[:, :, None], (local_tokens, 2, piece_rows)
        ).reshape(local_tokens, 2 * piece_rows)
        allowed = jnp.concatenate([suffix_allowed, prefix_allowed], axis=1)[:, None, :]
        values = jnp.concatenate(
            [
                suffix_keys[:, :latent_width],
                prefix_piece[:, :, :latent_width].reshape(2 * piece_rows, latent_width),
            ],
            axis=0,
        )
        return merge_scores(running_state, scores, allowed, values)

    final_max, final_sum, final_acc = lax.cond(single_prefix, one_prefix, two_prefixes, start_state)
    latent_out = (final_acc / final_sum[:, :, None]).astype(jnp.bfloat16)
    value_out = jnp.einsum(
        "thl,hlv->thv", latent_out, value_up, preferred_element_type=jnp.float32
    ).astype(jnp.bfloat16)
    value_out = value_out.reshape(local_tokens, head_count * value_up.shape[2])
    projected = jnp.dot(
        value_out,
        lax.all_gather(out_proj, "expert", axis=1, tiled=True),
        preferred_element_type=jnp.float32,
    )
    residual = hidden[0].astype(jnp.float32) + projected
    normed = (
        residual
        * lax.rsqrt(jnp.mean(residual * residual, axis=1, keepdims=True) + 1e-06)
        * norm_gain
    ).astype(jnp.bfloat16)
    logits = jnp.dot(normed, router, preferred_element_type=jnp.float32)
    expert_probs = jax.nn.softmax(logits, axis=1)
    expert_ids = jnp.arange(expert_count, dtype=jnp.int32)
    my_routes = routes[0]
    matches = my_routes[:, :, None] == expert_ids[None, None, :]
    gate_values = jnp.sum(jnp.where(matches, expert_probs[:, None, :], 0.0), axis=2)
    flat_hits = matches.reshape(local_tokens * top_count, expert_count).astype(jnp.int32)
    earlier = jnp.cumsum(flat_hits, axis=0) - flat_hits
    slot_index = jnp.sum(earlier * flat_hits, axis=1).reshape(local_tokens, top_count)
    cell_index = my_routes * capacity + slot_index
    cell_ids = jnp.arange(expert_count * capacity, dtype=jnp.int32)
    placing = jnp.sum(
        (cell_ids[:, None, None] == cell_index[None, :, :]).astype(jnp.int32), axis=2
    ).astype(jnp.bfloat16)
    outgoing = jnp.dot(placing, normed, preferred_element_type=jnp.float32).astype(jnp.bfloat16)
    outgoing = outgoing.reshape(expert_count, capacity, model_width)
    incoming = lax.all_to_all(outgoing, "expert", split_axis=0, concat_axis=0, tiled=True)
    full_in, full_out = (
        lax.all_gather(expert_in, "seq", axis=1, tiled=True),
        lax.all_gather(expert_out, "seq", axis=1, tiled=True),
    )
    all_rows = incoming.reshape(-1, model_width)
    gate_up = jnp.dot(all_rows, full_in[0], preferred_element_type=jnp.float32)
    hidden_units = gate_up.shape[1] // 2
    active = (jax.nn.silu(gate_up[:, :hidden_units]) * gate_up[:, hidden_units:]).astype(
        jnp.bfloat16
    )
    produced = lax.dot_general(
        active, full_out[0], (((1,), (1,)), ((), ())), preferred_element_type=jnp.float32
    ).astype(jnp.bfloat16)
    returned = lax.all_to_all(
        produced.reshape(-1, capacity, model_width),
        "expert",
        split_axis=0,
        concat_axis=0,
        tiled=True,
    )
    returned_rows = returned.reshape(-1, model_width)
    picked = returned_rows[cell_index]
    routed_sum = jnp.sum(gate_values[:, :, None] * picked.astype(jnp.float32), axis=1)
    layer_out = (residual + routed_sum).astype(jnp.bfloat16)
    return layer_out[None]


def solution(mesh):
    in_specs = (
        P("expert", "seq", None),
        P("expert", "seq", None),
        P("expert", "seq", None),
        P(None, "seq", None),
        P("expert", None),
        P("expert", None),
        P(),
        P(None, "expert"),
        P(),
        P(),
        P("expert", "seq", None),
        P("expert", "seq", None),
        P("expert", "seq", None),
    )
    out_specs = P("expert", "seq", None)
    return jax.shard_map(local, mesh=mesh, in_specs=in_specs, out_specs=out_specs, check_vma=False)
```

profile of v0, /device:TPU:16, one launch (start us, length us, event | category | flops | bytes accessed | tf_op | source)
XLA Modules:
  0.0 368.0 jit_solution(16596417180253832410)
XLA Ops:
  7.3 1.8 copy.86
  13.9 2.4 reshape_squeeze.3
  20.0 36.3 %all-gather.8.cloned.1.call-done = bf16[1,1024,576]{2,1,0:T(8,128)(2,1)} async-done(((bf16[1,64,576]{2,1,0:T(8,128)(2,1)}), bf16[1,1024,576]{2,1,0:T(8,128)(2,1)}) %all-gather.8.cloned.1.call-update) | async-done | bytes 1179664 | tf_op jit(solution)/shard_map/all_gather | solution.py:65
  56.3 2.4 copy.87
  58.7 2.5 convolution_multiply_fusion
  61.3 39.0 %all-gather.6.cloned.1.call-done = bf16[2,1024,576]{2,0,1:T(2,128)(2,1)} async-done(((bf16[2,64,576]{2,0,1:T(2,128)(2,1)}), bf16[2,1024,576]{2,0,1:T(2,128)(2,1)}) %all-gather.6.cloned.1.call-update) | async-done | bytes 2359312 | tf_op jit(solution)/shard_map/all_gather | solution.py:66
  100.3 31.3 %conditional.1 = (f32[64,8,512]{2,1,0:T(8,128)}, f32[64,8]{1,0:T(8,128)S(1)}) conditional(s32[]{:T(128)} %convert_element_type.64, (s32[64]{0:T(128)S(1)}, s32[64,2]{1,0:T(8,128)S(1)}, pred[64,1024]{1,0:T(8,128)(4,1)S(1)}, bf16[64,8,576]{2,1,0:T(8,128)(2,1)}, bf16[2,1024,576]{2,0,1:T(2,128)(2,1)}, /*index=5*/f32[64,8,1024]{2,1,0:T(8,128)S(1)}, ...), branch_computations={%region_5.8_spmd, %region_8.11_spmd} | conditional | flops 2843409920 | bytes 92157032 | solution.py:116
  100.3 7.4 %copy.88 = bf16[2,1024,576]{1,2,0:T(8,128)(2,1)} copy(bf16[2,1024,576]{2,0,1:T(2,128)(2,1)} %get-tuple-element.110) | data formatting | bytes 4718592 | tf_op jit(solution)/shard_map
  107.6 3.7 fusion.10
  111.7 1.2 select_reduce_fusion
  114.5 1.5 slice.36
  116.0 4.0 %copy.82 = bf16[2,1024,512]{2,1,0:T(8,128)(2,1)} copy(bf16[2,1024,512]{1,2,0:T(8,128)(2,1)} %slice.36) | data formatting | bytes 4194304 | tf_op jit(solution)/shard_map/cond/branch_0_fun/slice | solution.py:110
  120.0 2.4 copy.89
  122.4 1.3 slice.35
  123.7 5.9 %fusion.2 = f32[64,8,512]{2,1,0:T(8,128)} fusion(bf16[2048,512]{1,0:T(8,128)(2,1)} %bitcast.104, bf16[1024,512]{1,0:T(8,128)(2,1)S(1)} %slice.35, f32[64,8,2048]{2,1,0:T(8,128)} %bitcast.98, f32[64,8,1024]{2,1,0:T(8,128)S(1)} %get-tuple-element.36, f32[64,8]{1,0:T(8,128)S(1)} %broadcast_maximum_fusion, pred[64,3072]{1,0:T(8,128)(4,1)S(1)} %pad_add_fusion), kind=kOutput, calls=%fused_computation.7 | convolution fusion | flops 1623195648 | bytes 10684416 | tf_op jit(solution)/shard_map/cond/branch_0_fun/thn,nl->thl/dot_general | solution.py:19
  129.6 1.8 fusion.1
  131.5 1.4 divide_convert_fusion
  133.4 54.2 %all-gather.10.cloned.1.call-done = bf16[1024,2048]{0,1:T(8,128)(2,1)} async-done(((bf16[1024,64]{0,1:T(8,128)(2,1)}), bf16[1024,2048]{0,1:T(8,128)(2,1)}) %all-gather.10.cloned.1.call-update) | async-done | bytes 4194320 | tf_op jit(solution)/shard_map/all_gather | solution.py:124
  187.6 3.7 %multiply_reduce_fusion.1 = (f32[64]{0:T(128)S(1)}, f32[64,2048]{1,0:T(8,128)S(1)}) fusion(bf16[1024,2048]{0,1:T(8,128)(2,1)} %all-gather.10.cloned.1.call-done, bf16[8,8,8,128]{3,2,1,0:T(8,128)(2,1)S(1)} %fusion.33, bf16[1,64,2048]{2,1,0:T(8,128)(2,1)S(1)} %copy-done.9), kind=kOutput, calls=%fused_computation.60 | convolution fusion | flops 268959680 | bytes 5112064 | tf_op jit(solution)/shard_map/dot_general | solution.py:122
  192.1 2.1 convolution_convert_fusion.1
  194.1 7.2 %all-to-all-start = ((bf16[32,16,2048]{2,1,0:T(8,128)(2,1)}), bf16[32,16,2048]{2,1,0:T(8,128)(2,1)S(1)}, u32[]{:S(2)}, u32[]{:S(2)}) async-start(bf16[32,16,2048]{2,1,0:T(8,128)(2,1)} %bitcast.20), calls=%async_computation | async-start | bytes 4194304 | tf_op jit(solution)/shard_map/all_to_all | solution.py:149
  201.3 34.9 %all-gather.12.cloned.1.call-done = bf16[1,2048,1408]{2,1,0:T(8,128)(2,1)} async-done(((bf16[1,128,1408]{2,1,0:T(8,128)(2,1)}), bf16[1,2048,1408]{2,1,0:T(8,128)(2,1)}) %all-gather.12.cloned.1.call-update) | async-done | bytes 5767184 | tf_op jit(solution)/shard_map/all_gather | solution.py:151
  236.2 11.3 %all-to-all-done = bf16[32,16,2048]{2,1,0:T(8,128)(2,1)S(1)} async-done(((bf16[32,16,2048]{2,1,0:T(8,128)(2,1)}), bf16[32,16,2048]{2,1,0:T(8,128)(2,1)S(1)}, u32[]{:S(2)}, u32[]{:S(2)}) %all-to-all-start) | async-done | bytes 2097184 | tf_op jit(solution)/shard_map/all_to_all | solution.py:149
  247.5 7.6 %fusion.28 = f32[512,1408]{1,0:T(8,128)} fusion(bf16[512,2048]{1,0:T(8,128)(2,1)S(1)} %bitcast.103, bf16[1,2048,1408]{2,1,0:T(8,128)(2,1)} %all-gather.12.cloned.1.call-done), kind=kOutput, calls=%fused_computation.40 | convolution fusion | flops 2952790016 | bytes 10747904 | tf_op jit(solution)/shard_map/dot_general | solution.py:155
  255.2 28.3 %all-gather.14.cloned.1.call-done = bf16[1,2048,704]{1,2,0:T(8,128)(2,1)} async-done(((bf16[1,128,704]{1,2,0:T(8,128)(2,1)}), bf16[1,2048,704]{1,2,0:T(8,128)(2,1)}) %all-gather.14.cloned.1.call-update) | async-done | bytes 2883600 | tf_op jit(solution)/shard_map/all_gather | solution.py:152
  283.5 6.0 %convolution_convert_fusion = bf16[512,2048]{1,0:T(8,128)(2,1)} fusion(bf16[1,2048,704]{1,2,0:T(8,128)(2,1)} %all-gather.14.cloned.1.call-done, f32[512,1408]{1,0:T(8,128)} %fusion.28), kind=kOutput, calls=%fused_computation.43 | convolution fusion | flops 1479606272 | bytes 8126464 | tf_op jit(solution)/shard_map/dot_general | solution.py:160
  289.5 10.0 %all-to-all-start.1 = ((bf16[32,16,2048]{2,1,0:T(8,128)(2,1)}), bf16[32,16,2048]{2,1,0:T(8,128)(2,1)S(1)}, u32[]{:S(2)}, u32[]{:S(2)}) async-start(bf16[32,16,2048]{2,1,0:T(8,128)(2,1)} %bitcast.102), calls=%async_computation.1 | async-start | bytes 4194304 | tf_op jit(solution)/shard_map/all_to_all | solution.py:163
  299.8 1.3 fusion.50
  301.3 48.6 %all-to-all-done.1 = bf16[32,16,2048]{2,1,0:T(8,128)(2,1)S(1)} async-done(((bf16[32,16,2048]{2,1,0:T(8,128)(2,1)}), bf16[32,16,2048]{2,1,0:T(8,128)(2,1)S(1)}, u32[]{:S(2)}, u32[]{:S(2)}) %all-to-all-start.1) | async-done | bytes 2097184 | tf_op jit(solution)/shard_map/all_to_all | solution.py:163
  349.9 3.1 gather_fusion
  353.0 3.9 %reshape.155 = f32[64,6,2048]{2,1,0:T(8,128)} reshape(bf16[384,2048]{1,0:T(8,128)(2,1)} %gather_fusion) | data formatting | bytes 4718592 | tf_op jit(solution)/shard_map/convert_element_type | solution.py:172
  356.9 3.8 %multiply_reduce_fusion = f32[64,2048]{1,0:T(8,128)S(1)} fusion(f32[64,6,2048]{2,1,0:T(8,128)} %reshape.155, f32[64,6]{1,0:T(8,128)S(1)} %copy.96), kind=kLoop, calls=%fused_computation.42 | loop fusion | flops 1441792 | bytes 3671552 | tf_op jit(solution)/shard_map/reduce_sum | solution.py:172
  (69 shorter events, 12.9 us)
Async XLA Ops:
  6.5 126.4 %copy-start = (bf16[8,512,128]{2,1,0:T(8,128)(2,1)S(1)}, bf16[8,512,128]{2,1,0:T(8,128)(2,1)}, u32[]{:S(2)}) copy-start(bf16[8,512,128]{2,1,0:T(8,128)(2,1)} %param.21) | copy-start | bytes 3145732
  6.5 49.8 %all-gather.8.cloned.1.call-start = ((), (), s32[]{:S(2)}) async-start(), calls=%async_computation.3 | async-start | bytes 1392640 | tf_op jit(solution)/shard_map/all_gather | solution.py:65
  7.3 93.0 %all-gather.6.cloned.1.call-start = ((), (), s32[]{:S(2)}) async-start(), calls=%async_computation.2 | async-start | bytes 2785280 | tf_op jit(solution)/shard_map/all_gather | solution.py:66
  9.1 178.5 %all-gather.10.cloned.1.call-start = ((), (), s32[]{:S(2)}) async-start(), calls=%async_computation.4 | async-start | bytes 4325376 | tf_op jit(solution)/shard_map/all_gather | solution.py:124
  9.8 226.4 %all-gather.12.cloned.1.call-start = ((), (), s32[]{:S(2)}) async-start(), calls=%async_computation.5 | async-start | bytes 6127616 | tf_op jit(solution)/shard_map/all_gather | solution.py:151
  10.4 273.1 %all-gather.14.cloned.1.call-start = ((), (), s32[]{:S(2)}) async-start(), calls=%async_computation.6 | async-start | bytes 3063808 | tf_op jit(solution)/shard_map/all_gather | solution.py:152
  111.3 2.1 copy-start.1
  111.7 2.7 copy-start.4
  123.7 5.9 %copy-start.2 = (f32[64,8,2,1024]{3,1,2,0:T(8,128)S(1)}, f32[64,8,2,1024]{3,1,2,0:T(8,128)}, u32[]{:S(2)}) copy-start(f32[64,8,2,1024]{3,1,2,0:T(8,128)} %copy-done.1) | copy-start | bytes 12582916 | tf_op jit(solution)/shard_map/cond
  131.5 56.0 %copy-start.9 = (bf16[1,64,2048]{2,1,0:T(8,128)(2,1)S(1)}, bf16[1,64,2048]{2,1,0:T(8,128)(2,1)}, u32[]{:S(2)}) copy-start(bf16[1,64,2048]{2,1,0:T(8,128)(2,1)} %param.15) | copy-start | bytes 786436
  133.3 58.7 %copy-start.8 = (s32[512,64]{0,1:T(8,128)S(1)}, s32[512,64]{0,1:T(8,128)}, u32[]{:S(2)}) copy-start(s32[512,64]{0,1:T(8,128)} %convert_reduce_fusion) | copy-start | bytes 393220
  133.3 58.7 %copy-start.11 = (f32[2048]{0:T(1024)S(1)}, f32[2048]{0:T(1024)}, u32[]{:S(2)}) copy-start(f32[2048]{0:T(1024)} %param.23) | copy-start | bytes 24580
  191.2 0.8 copy-start.5
  194.1 53.4 %all-to-all-start = ((bf16[32,16,2048]{2,1,0:T(8,128)(2,1)}), bf16[32,16,2048]{2,1,0:T(8,128)(2,1)S(1)}, u32[]{:S(2)}, u32[]{:S(2)}) async-start(bf16[32,16,2048]{2,1,0:T(8,128)(2,1)} %bitcast.20), calls=%async_computation | async-start | bytes 4194304 | tf_op jit(solution)/shard_map/all_to_all | solution.py:149
  289.5 10.0 %copy-start.12 = (s32[1,64,6]{1,0,2:T(1,128)S(1)}, s32[1,64,6]{1,0,2:T(1,128)}, u32[]{:S(2)}) copy-start(s32[1,64,6]{1,0,2:T(1,128)} %param.25) | copy-start | bytes 4612
  289.5 10.3 %copy-start.10 = (bf16[2048,32]{0,1:T(8,128)(2,1)S(1)}, bf16[2048,32]{0,1:T(8,128)(2,1)}, u32[]{:S(2)}) copy-start(bf16[2048,32]{0,1:T(8,128)(2,1)} %param.24) | copy-start | bytes 393220
  289.5 60.4 %all-to-all-start.1 = ((bf16[32,16,2048]{2,1,0:T(8,128)(2,1)}), bf16[32,16,2048]{2,1,0:T(8,128)(2,1)S(1)}, u32[]{:S(2)}, u32[]{:S(2)}) async-start(bf16[32,16,2048]{2,1,0:T(8,128)(2,1)} %bitcast.102), calls=%async_computation.1 | async-start | bytes 4194304 | tf_op jit(solution)/shard_map/all_to_all | solution.py:163
  356.9 3.8 %copy-start.6 = (f32[64,2048]{1,0:T(8,128)S(1)}, f32[64,2048]{1,0:T(8,128)}, u32[]{:S(2)}) copy-start(f32[64,2048]{1,0:T(8,128)} %copy-done.5) | copy-start | bytes 1572868
Sparse Core Ops, SparseCore 0:
  9.5 46.7 all-gather.7
  58.4 41.7 all-gather.5
  103.4 84.0 all-gather.9
  189.5 46.6 all-gather.11
  238.1 45.3 all-gather.13
where the time goes:
time: 369 us; the launch traced here: 368 us
  waiting for transfers between devices  255 us (69%)
  local copies, waits for them, and re-layouts  34.7 us (9%)
  matrix products  33.2 us (9%)
  starting transfers between devices  17.3 us (5%)
  between operations  14 us (4%)
  other arithmetic  13.5 us (4%)
    all_gather x1, waiting for transfers between devices, local(): lax.all_gather(out_proj, 'expert', axis=1, tiled=True)  54.2 us
    all_to_all x1, waiting for transfers between devices, local(): lax.all_to_all(produced.reshape(-1, capacity, model_width), 'expert', spl...  48.6 us
    all_gather x1, waiting for transfers between devices, local(): prefix_piece = lax.all_gather(prefix_latent, 'seq', axis=1, tiled=True)  39 us
    all_gather x1, waiting for transfers between devices, local(): suffix_piece = lax.all_gather(suffix_latent, 'seq', axis=1, tiled=True)  36.3 us
    all_gather x1, waiting for transfers between devices, local(): lax.all_gather(expert_in, 'seq', axis=1, tiled=True)  34.9 us
    all_gather x1, waiting for transfers between devices, local(): lax.all_gather(expert_out, 'seq', axis=1, tiled=True)  28.3 us
    all_to_all x1, waiting for transfers between devices, local(): lax.all_to_all(outgoing, 'expert', split_axis=0, concat_axis=0, tiled=True)  11.3 us
    all_to_all x1, starting transfers between devices, local(): lax.all_to_all(produced.reshape(-1, capacity, model_width), 'expert', spl...  9.96 us
  transfers between devices with their start and end apart: 7, of which 7 were waited for; matrix products, arithmetic and copies ran while one was open for 17% of the time, Pallas kernels for 0%

commit v1 on v0

--- a/solution.py
+++ b/solution.py
@@ -1,3 +1,4 @@
+import functools
 import jax
 import jax.numpy as jnp
 from jax import lax
@@ -5,6 +6,22 @@
 
 qk_scale = 192.0 ** (-0.5)
 big_negative = -1e30
+
+
+def create_groups_for(point, on_dim):
+    q_n = lax.axis_size("seq")
+    pool = tuple(((i0, (i0 + 1) % q_n) for i0 in range(q_n)))
+
+    def apply_the_units(val):
+        if len(val) == q_n:
+            return val
+        return apply_the_units([lax.ppermute(val[0], axis_name="seq", perm=pool), *val])
+
+    v_now = jnp.concatenate(apply_the_units([point]), axis=on_dim)
+    return jnp.roll(v_now, (lax.axis_index("seq") + 1) * point.shape[on_dim], axis=on_dim)
+
+
+order_run = functools.partial(create_groups_for, on_dim=1)
 
 
 def request_of(positions, request_ends):
@@ -63,7 +80,7 @@
         jnp.zeros((local_tokens, head_count, latent_width), jnp.float32),
     )
     suffix_piece = lax.all_gather(suffix_latent, "seq", axis=1, tiled=True)
-    prefix_piece = lax.all_gather(prefix_latent, "seq", axis=1, tiled=True)
+    prefix_piece = order_run(prefix_latent)
     piece_rows = suffix_piece.shape[1]
     suffix_keys = suffix_piece[0]
     key_positions = jnp.arange(piece_rows, dtype=jnp.int32)

time: 369 us -> 326 us (0.88)
  waiting for transfers between devices: 255 us -> 197 us
  local copies, waits for them, and re-layouts: 34.7 us -> 49.1 us
    ppermute x0 -> x15, waiting for transfers between devices: none -> 104 us  [apply_the_units(): lax.ppermute(val[0], axis_name='seq', perm=pool)]
    all_gather x1, waiting for transfers between devices: 54.2 us -> 0.02 us  [local(): lax.all_gather(out_proj, 'expert', axis=1, tiled=True)]
    all_gather x1 -> x0, waiting for transfers between devices: 39 us -> none  [local(): prefix_piece = lax.all_gather(prefix_latent, 'seq', axis=1, tiled=True)]
    all_gather x1, waiting for transfers between devices: 36.3 us -> 0.02 us  [local(): suffix_piece = lax.all_gather(suffix_latent, 'seq', axis=1, tiled=True)]
    all_gather x1, waiting for transfers between devices: 34.9 us -> 2.2 us  [local(): lax.all_gather(expert_in, 'seq', axis=1, tiled=True)]
    all_gather x1, waiting for transfers between devices: 28.3 us -> 2.12 us  [local(): lax.all_gather(expert_out, 'seq', axis=1, tiled=True)]
    all_to_all x1, waiting for transfers between devices: 11.3 us -> 37.2 us  [local(): lax.all_to_all(outgoing, 'expert', split_axis=0, concat_axis=0, tiled=True)]
    concatenate x0 -> x1, local copies, waits for them, and re-layouts: none -> 13.1 us  [create_groups_for(): jnp.roll(v_now, (lax.axis_index('seq') + 1) * point.shape[on_dim], axis=o...]
  transfers between devices with their start and end apart: 7 -> 21, of which waited for: 7 -> 19; matrix products, arithmetic and copies ran while one was open for 17% -> 22% of each run, Pallas kernels for 0% -> 0%
where the time goes in v1:
time: 326 us; the launch traced here: 324 us
  waiting for transfers between devices  197 us (60%)
  local copies, waits for them, and re-layouts  49.1 us (15%)
  matrix products  33.5 us (10%)
  starting transfers between devices  17.3 us (5%)
  between operations  14.1 us (4%)
  other arithmetic  13.6 us (4%)
    ppermute x15, waiting for transfers between devices, apply_the_units(): lax.ppermute(val[0], axis_name='seq', perm=pool)  104 us
    all_to_all x1, waiting for transfers between devices, local(): lax.all_to_all(produced.reshape(-1, capacity, model_width), 'expert', spl...  48.6 us
    all_to_all x1, waiting for transfers between devices, local(): lax.all_to_all(outgoing, 'expert', split_axis=0, concat_axis=0, tiled=True)  37.2 us
    concatenate x1, local copies, waits for them, and re-layouts, create_groups_for(): jnp.roll(v_now, (lax.axis_index('seq') + 1) * point.shape[on_dim], axis=o...  13.1 us
    all_to_all x1, starting transfers between devices, local(): lax.all_to_all(produced.reshape(-1, capacity, model_width), 'expert', spl...  9.96 us
    dot_general x1, matrix products, local(): gate_up = jnp.dot(all_rows, full_in[0], preferred_element_type=jnp.float32)  7.75 us
    unnamed x45, local copies, waits for them, and re-layouts  7.17 us
    all_to_all x1, starting transfers between devices, local(): lax.all_to_all(outgoing, 'expert', split_axis=0, concat_axis=0, tiled=True)  7.16 us
  transfers between devices with their start and end apart: 21, of which 19 were waited for; matrix products, arithmetic and copies ran while one was open for 22% of the time, Pallas kernels for 0%

profile of v1, /device:TPU:16, one launch (start us, length us, event | category | flops | bytes accessed | tf_op | source)
XLA Modules:
  0.0 324.2 jit_solution(1581888031089553037)
XLA Ops:
  9.9 12.9 %collective-permute-done = bf16[2,64,576]{1,2,0:T(8,128)(2,1)S(1)} collective-permute-done((bf16[2,64,576]{1,2,0:T(8,128)(2,1)S(1)}, bf16[2,64,576]{1,2,0:T(8,128)(2,1)S(1)}, u32[]{:S(2)}, u32[]{:S(2)}) %collective-permute-start) | collective-permute-done | bytes 147488 | tf_op jit(solution)/shard_map/ppermute | solution.py:18
  23.5 7.4 %collective-permute-done.1 = bf16[2,64,576]{1,2,0:T(8,128)(2,1)S(1)} collective-permute-done((bf16[2,64,576]{1,2,0:T(8,128)(2,1)S(1)}, bf16[2,64,576]{1,2,0:T(8,128)(2,1)S(1)}, u32[]{:S(2)}, u32[]{:S(2)}) %collective-permute-start.1) | collective-permute-done | bytes 147488 | tf_op jit(solution)/shard_map/ppermute | solution.py:18
  31.6 8.3 %collective-permute-done.2 = bf16[2,64,576]{1,2,0:T(8,128)(2,1)S(1)} collective-permute-done((bf16[2,64,576]{1,2,0:T(8,128)(2,1)S(1)}, bf16[2,64,576]{1,2,0:T(8,128)(2,1)S(1)}, u32[]{:S(2)}, u32[]{:S(2)}) %collective-permute-start.2) | collective-permute-done | bytes 147488 | tf_op jit(solution)/shard_map/ppermute | solution.py:18
  40.7 8.2 %collective-permute-done.3 = bf16[2,64,576]{1,2,0:T(8,128)(2,1)S(1)} collective-permute-done((bf16[2,64,576]{1,2,0:T(8,128)(2,1)S(1)}, bf16[2,64,576]{1,2,0:T(8,128)(2,1)S(1)}, u32[]{:S(2)}, u32[]{:S(2)}) %collective-permute-start.3) | collective-permute-done | bytes 147488 | tf_op jit(solution)/shard_map/ppermute | solution.py:18
  49.7 7.6 %collective-permute-done.4 = bf16[2,64,576]{1,2,0:T(8,128)(2,1)S(1)} collective-permute-done((bf16[2,64,576]{1,2,0:T(8,128)(2,1)S(1)}, bf16[2,64,576]{1,2,0:T(8,128)(2,1)S(1)}, u32[]{:S(2)}, u32[]{:S(2)}) %collective-permute-start.4) | collective-permute-done | bytes 147488 | tf_op jit(solution)/shard_map/ppermute | solution.py:18
  58.0 7.4 %collective-permute-done.5 = bf16[2,64,576]{1,2,0:T(8,128)(2,1)S(1)} collective-permute-done((bf16[2,64,576]{1,2,0:T(8,128)(2,1)S(1)}, bf16[2,64,576]{1,2,0:T(8,128)(2,1)S(1)}, u32[]{:S(2)}, u32[]{:S(2)}) %collective-permute-start.5) | collective-permute-done | bytes 147488 | tf_op jit(solution)/shard_map/ppermute | solution.py:18
  66.0 7.4 %collective-permute-done.6 = bf16[2,64,576]{1,2,0:T(8,128)(2,1)S(1)} collective-permute-done((bf16[2,64,576]{1,2,0:T(8,128)(2,1)S(1)}, bf16[2,64,576]{1,2,0:T(8,128)(2,1)S(1)}, u32[]{:S(2)}, u32[]{:S(2)}) %collective-permute-start.6) | collective-permute-done | bytes 147488 | tf_op jit(solution)/shard_map/ppermute | solution.py:18
  74.4 6.4 %collective-permute-done.7 = bf16[2,64,576]{1,2,0:T(8,128)(2,1)S(1)} collective-permute-done((bf16[2,64,576]{1,2,0:T(8,128)(2,1)S(1)}, bf16[2,64,576]{1,2,0:T(8,128)(2,1)S(1)}, u32[]{:S(2)}, u32[]{:S(2)}) %collective-permute-start.7) | collective-permute-done | bytes 147488 | tf_op jit(solution)/shard_map/ppermute | solution.py:18
  81.7 6.5 %collective-permute-done.8 = bf16[2,64,576]{1,2,0:T(8,128)(2,1)S(1)} collective-permute-done((bf16[2,64,576]{1,2,0:T(8,128)(2,1)S(1)}, bf16[2,64,576]{1,2,0:T(8,128)(2,1)S(1)}, u32[]{:S(2)}, u32[]{:S(2)}) %collective-permute-start.8) | collective-permute-done | bytes 147488 | tf_op jit(solution)/shard_map/ppermute | solution.py:18
  88.8 6.7 %collective-permute-done.9 = bf16[2,64,576]{1,2,0:T(8,128)(2,1)S(1)} collective-permute-done((bf16[2,64,576]{1,2,0:T(8,128)(2,1)S(1)}, bf16[2,64,576]{1,2,0:T(8,128)(2,1)S(1)}, u32[]{:S(2)}, u32[]{:S(2)}) %collective-permute-start.9) | collective-permute-done | bytes 147488 | tf_op jit(solution)/shard_map/ppermute | solution.py:18
  96.5 6.4 %collective-permute-done.10 = bf16[2,64,576]{1,2,0:T(8,128)(2,1)S(1)} collective-permute-done((bf16[2,64,576]{1,2,0:T(8,128)(2,1)S(1)}, bf16[2,64,576]{1,2,0:T(8,128)(2,1)S(1)}, u32[]{:S(2)}, u32[]{:S(2)}) %collective-permute-start.10) | collective-permute-done | bytes 147488 | tf_op jit(solution)/shard_map/ppermute | solution.py:18
  102.9 7.3 %collective-permute-done.11 = bf16[2,64,576]{1,2,0:T(8,128)(2,1)S(1)} collective-permute-done((bf16[2,64,576]{1,2,0:T(8,128)(2,1)S(1)}, bf16[2,64,576]{1,2,0:T(8,128)(2,1)S(1)}, u32[]{:S(2)}, u32[]{:S(2)}) %collective-permute-start.11) | collective-permute-done | bytes 147488 | tf_op jit(solution)/shard_map/ppermute | solution.py:18
  111.1 6.5 %collective-permute-done.12 = bf16[2,64,576]{1,2,0:T(8,128)(2,1)S(1)} collective-permute-done((bf16[2,64,576]{1,2,0:T(8,128)(2,1)S(1)}, bf16[2,64,576]{1,2,0:T(8,128)(2,1)S(1)}, u32[]{:S(2)}, u32[]{:S(2)}) %collective-permute-start.12) | collective-permute-done | bytes 147488 | tf_op jit(solution)/shard_map/ppermute | solution.py:18
  122.2 2.8 collective-permute-done.13
  130.1 2.6 collective-permute-done.14
  132.7 13.1 %concatenate.24 = bf16[2,2048,576]{1,2,0:T(8,128)(2,1)} concatenate(bf16[2,64,576]{1,2,0:T(8,128)(2,1)} %collective-permute-done.14, bf16[2,64,576]{1,2,0:T(8,128)(2,1)} %collective-permute-done.13, bf16[2,64,576]{1,2,0:T(8,128)(2,1)} %copy-done.18, bf16[2,64,576]{1,2,0:T(8,128)(2,1)} %copy-done.17, bf16[2,64,576]{1,2,0:T(8,128)(2,1)} %copy-done.16, ...), dimensions={1} | concatenate | bytes 9437184 | tf_op jit(solution)/shard_map/jit(_roll_dynamic)/concatenate | solution.py:21
  145.8 4.3 %constant_dynamic-slice_fusion = bf16[2,1024,576]{1,2,0:T(8,128)(2,1)} fusion(bf16[2,2048,576]{1,2,0:T(8,128)(2,1)} %concatenate.24, s32[]{:T(128)S(6)} %select_n.51), kind=kLoop, calls=%fused_computation.94 | loop fusion | bytes 4718596 | tf_op jit(solution)/shard_map/jit(_roll_dynamic)/dynamic_slice | solution.py:21
  150.1 24.5 %conditional.1 = (f32[64,8,512]{2,1,0:T(8,128)}, f32[64,8]{1,0:T(8,128)S(1)}) conditional(s32[]{:T(128)} %convert_element_type.64, (s32[64]{0:T(128)S(1)}, s32[64,2]{1,0:T(8,128)S(1)}, pred[64,1024]{1,0:T(8,128)(4,1)S(1)}, bf16[64,8,576]{2,1,0:T(8,128)(2,1)}, bf16[2,1024,576]{1,2,0:T(8,128)(2,1)}, /*index=5*/f32[64,8,1024]{2,1,0:T(8,128)S(1)}, ...), branch_computations={%region_5.8_spmd, %region_8.11_spmd} | conditional | flops 2843409920 | bytes 78001224 | solution.py:133
  150.1 3.7 %fusion.10 = f32[64,8,2,1024]{3,1,2,0:T(8,128)S(1)} fusion(bf16[2,1024,576]{1,2,0:T(8,128)(2,1)} %get-tuple-element.38, bf16[64,8,576]{2,1,0:T(8,128)(2,1)} %get-tuple-element.37), kind=kOutput, calls=%fused_computation.14 | convolution fusion | flops 1209008128 | bytes 7143424 | tf_op jit(solution)/shard_map/cond/branch_0_fun/thk,pnk->thpn/dot_general | solution.py:112
  155.9 3.1 slice.20
  159.0 4.0 %copy.86 = bf16[2,1024,512]{2,1,0:T(8,128)(2,1)} copy(bf16[2,1024,512]{1,2,0:T(8,128)(2,1)} %slice.20) | data formatting | bytes 4194304 | tf_op jit(solution)/shard_map/cond/branch_0_fun/slice | solution.py:127
  166.7 6.0 %fusion.2 = f32[64,8,512]{2,1,0:T(8,128)} fusion(bf16[2048,512]{1,0:T(8,128)(2,1)} %bitcast.104, bf16[1024,512]{1,0:T(8,128)(2,1)S(1)} %slice.35, f32[64,8,2048]{2,1,0:T(8,128)} %bitcast.98, f32[64,8,1024]{2,1,0:T(8,128)S(1)} %get-tuple-element.36, f32[64,8]{1,0:T(8,128)S(1)} %broadcast_maximum_fusion, pred[64,3072]{1,0:T(8,128)(4,1)S(1)} %pad_add_fusion), kind=kOutput, calls=%fused_computation.7 | convolution fusion | flops 1623195648 | bytes 10684416 | tf_op jit(solution)/shard_map/cond/branch_0_fun/thn,nl->thl/dot_general | solution.py:36
  176.5 3.8 %multiply_reduce_fusion.1 = (f32[64]{0:T(128)S(1)}, f32[64,2048]{1,0:T(8,128)S(1)}) fusion(bf16[1024,2048]{0,1:T(8,128)(2,1)} %all-gather.7.cloned.1.call-done, bf16[8,8,8,128]{3,2,1,0:T(8,128)(2,1)S(1)} %fusion.33, bf16[1,64,2048]{2,1,0:T(8,128)(2,1)S(1)} %copy-done.20), kind=kOutput, calls=%fused_computation.60 | convolution fusion | flops 268959680 | bytes 5112064 | tf_op jit(solution)/shard_map/dot_general | solution.py:139
  183.3 7.2 %all-to-all-start = ((bf16[32,16,2048]{2,1,0:T(8,128)(2,1)}), bf16[32,16,2048]{2,1,0:T(8,128)(2,1)S(1)}, u32[]{:S(2)}, u32[]{:S(2)}) async-start(bf16[32,16,2048]{2,1,0:T(8,128)(2,1)} %bitcast.20), calls=%async_computation | async-start | bytes 4194304 | tf_op jit(solution)/shard_map/all_to_all | solution.py:166
  192.6 37.2 %all-to-all-done = bf16[32,16,2048]{2,1,0:T(8,128)(2,1)S(1)} async-done(((bf16[32,16,2048]{2,1,0:T(8,128)(2,1)}), bf16[32,16,2048]{2,1,0:T(8,128)(2,1)S(1)}, u32[]{:S(2)}, u32[]{:S(2)}) %all-to-all-start) | async-done | bytes 2097184 | tf_op jit(solution)/shard_map/all_to_all | solution.py:166
  229.9 7.8 %fusion.28 = f32[512,1408]{1,0:T(8,128)} fusion(bf16[512,2048]{1,0:T(8,128)(2,1)S(1)} %bitcast.103, bf16[1,2048,1408]{2,1,0:T(8,128)(2,1)} %all-gather.9.cloned.1.call-done), kind=kOutput, calls=%fused_computation.40 | convolution fusion | flops 2952790016 | bytes 10747904 | tf_op jit(solution)/shard_map/dot_general | solution.py:172
  239.7 6.0 %convolution_convert_fusion = bf16[512,2048]{1,0:T(8,128)(2,1)} fusion(bf16[1,2048,704]{1,2,0:T(8,128)(2,1)} %all-gather.11.cloned.1.call-done, f32[512,1408]{1,0:T(8,128)} %fusion.28), kind=kOutput, calls=%fused_computation.43 | convolution fusion | flops 1479606272 | bytes 8126464 | tf_op jit(solution)/shard_map/dot_general | solution.py:177
  245.7 10.0 %all-to-all-start.1 = ((bf16[32,16,2048]{2,1,0:T(8,128)(2,1)}), bf16[32,16,2048]{2,1,0:T(8,128)(2,1)S(1)}, u32[]{:S(2)}, u32[]{:S(2)}) async-start(bf16[32,16,2048]{2,1,0:T(8,128)(2,1)} %bitcast.102), calls=%async_computation.1 | async-start | bytes 4194304 | tf_op jit(solution)/shard_map/all_to_all | solution.py:180
  257.5 48.6 %all-to-all-done.1 = bf16[32,16,2048]{2,1,0:T(8,128)(2,1)S(1)} async-done(((bf16[32,16,2048]{2,1,0:T(8,128)(2,1)}), bf16[32,16,2048]{2,1,0:T(8,128)(2,1)S(1)}, u32[]{:S(2)}, u32[]{:S(2)}) %all-to-all-start.1) | async-done | bytes 2097184 | tf_op jit(solution)/shard_map/all_to_all | solution.py:180
  306.1 3.1 gather_fusion
  309.2 3.9 %reshape.155 = f32[64,6,2048]{2,1,0:T(8,128)} reshape(bf16[384,2048]{1,0:T(8,128)(2,1)} %gather_fusion) | data formatting | bytes 4718592 | tf_op jit(solution)/shard_map/convert_element_type | solution.py:189
  313.1 3.8 %multiply_reduce_fusion = f32[64,2048]{1,0:T(8,128)S(1)} fusion(f32[64,6,2048]{2,1,0:T(8,128)} %reshape.155, f32[64,6]{1,0:T(8,128)S(1)} %copy.100), kind=kLoop, calls=%fused_computation.42 | loop fusion | flops 1441792 | bytes 3671552 | tf_op jit(solution)/shard_map/reduce_sum | solution.py:189
  (121 shorter events, 40.3 us)
Async XLA Ops:
  6.5 169.6 %copy-start = (bf16[8,512,128]{2,1,0:T(8,128)(2,1)S(1)}, bf16[8,512,128]{2,1,0:T(8,128)(2,1)}, u32[]{:S(2)}) copy-start(bf16[8,512,128]{2,1,0:T(8,128)(2,1)} %param.21) | copy-start | bytes 3145732
  6.5 118.6 %all-gather.5.cloned.1.call-start = ((), (), s32[]{:S(2)}) async-start(), calls=%async_computation.2 | async-start | bytes 1392640 | tf_op jit(solution)/shard_map/all_gather | solution.py:82
  7.3 169.3 %all-gather.7.cloned.1.call-start = ((), (), s32[]{:S(2)}) async-start(), calls=%async_computation.3 | async-start | bytes 4325376 | tf_op jit(solution)/shard_map/all_gather | solution.py:141
  8.0 184.6 %all-gather.9.cloned.1.call-start = ((), (), s32[]{:S(2)}) async-start(), calls=%async_computation.4 | async-start | bytes 6127616 | tf_op jit(solution)/shard_map/all_gather | solution.py:168
  8.7 231.0 %all-gather.11.cloned.1.call-start = ((), (), s32[]{:S(2)}) async-start(), calls=%async_computation.5 | async-start | bytes 3063808 | tf_op jit(solution)/shard_map/all_gather | solution.py:169
  9.9 12.9 %collective-permute-start = (bf16[2,64,576]{1,2,0:T(8,128)(2,1)S(1)}, bf16[2,64,576]{1,2,0:T(8,128)(2,1)S(1)}, u32[]{:S(2)}, u32[]{:S(2)}) collective-permute-start(bf16[2,64,576]{1,2,0:T(8,128)(2,1)S(1)} %copy.90), channel_id=1, source_target_pairs={{0,32},{32,64},{64,96},{96,128},{128,160},{160,192},{192,224},{224... | collective-permute-start | bytes 442376 | tf_op jit(solution)/shard_map/ppermute | solution.py:18
  23.5 7.4 %collective-permute-start.1 = (bf16[2,64,576]{1,2,0:T(8,128)(2,1)S(1)}, bf16[2,64,576]{1,2,0:T(8,128)(2,1)S(1)}, u32[]{:S(2)}, u32[]{:S(2)}) collective-permute-start(bf16[2,64,576]{1,2,0:T(8,128)(2,1)S(1)} %collective-permute-done), channel_id=1, source_target_pairs={{0,32},{32,64},{64,96},{96,128},{128,160},{160,192},{192,224},{224... | collective-permute-start | bytes 442376 | tf_op jit(solution)/shard_map/ppermute | solution.py:18
  31.6 8.3 %collective-permute-start.2 = (bf16[2,64,576]{1,2,0:T(8,128)(2,1)S(1)}, bf16[2,64,576]{1,2,0:T(8,128)(2,1)S(1)}, u32[]{:S(2)}, u32[]{:S(2)}) collective-permute-start(bf16[2,64,576]{1,2,0:T(8,128)(2,1)S(1)} %collective-permute-done.1), channel_id=1, source_target_pairs={{0,32},{32,64},{64,96},{96,128},{128,160},{160,192},{192,224},{224... | collective-permute-start | bytes 442376 | tf_op jit(solution)/shard_map/ppermute | solution.py:18
  40.7 8.2 %collective-permute-start.3 = (bf16[2,64,576]{1,2,0:T(8,128)(2,1)S(1)}, bf16[2,64,576]{1,2,0:T(8,128)(2,1)S(1)}, u32[]{:S(2)}, u32[]{:S(2)}) collective-permute-start(bf16[2,64,576]{1,2,0:T(8,128)(2,1)S(1)} %collective-permute-done.2), channel_id=1, source_target_pairs={{0,32},{32,64},{64,96},{96,128},{128,160},{160,192},{192,224},{224... | collective-permute-start | bytes 442376 | tf_op jit(solution)/shard_map/ppermute | solution.py:18
  49.6 7.6 %collective-permute-start.4 = (bf16[2,64,576]{1,2,0:T(8,128)(2,1)S(1)}, bf16[2,64,576]{1,2,0:T(8,128)(2,1)S(1)}, u32[]{:S(2)}, u32[]{:S(2)}) collective-permute-start(bf16[2,64,576]{1,2,0:T(8,128)(2,1)S(1)} %collective-permute-done.3), channel_id=1, source_target_pairs={{0,32},{32,64},{64,96},{96,128},{128,160},{160,192},{192,224},{224... | collective-permute-start | bytes 442376 | tf_op jit(solution)/shard_map/ppermute | solution.py:18
  58.0 7.4 %collective-permute-start.5 = (bf16[2,64,576]{1,2,0:T(8,128)(2,1)S(1)}, bf16[2,64,576]{1,2,0:T(8,128)(2,1)S(1)}, u32[]{:S(2)}, u32[]{:S(2)}) collective-permute-start(bf16[2,64,576]{1,2,0:T(8,128)(2,1)S(1)} %collective-permute-done.4), channel_id=1, source_target_pairs={{0,32},{32,64},{64,96},{96,128},{128,160},{160,192},{192,224},{224... | collective-permute-start | bytes 442376 | tf_op jit(solution)/shard_map/ppermute | solution.py:18
  66.0 7.4 %collective-permute-start.6 = (bf16[2,64,576]{1,2,0:T(8,128)(2,1)S(1)}, bf16[2,64,576]{1,2,0:T(8,128)(2,1)S(1)}, u32[]{:S(2)}, u32[]{:S(2)}) collective-permute-start(bf16[2,64,576]{1,2,0:T(8,128)(2,1)S(1)} %collective-permute-done.5), channel_id=1, source_target_pairs={{0,32},{32,64},{64,96},{96,128},{128,160},{160,192},{192,224},{224... | collective-permute-start | bytes 442376 | tf_op jit(solution)/shard_map/ppermute | solution.py:18
  73.4 51.6 %copy-start.12 = (bf16[2,64,576]{1,2,0:T(8,128)(2,1)}, bf16[2,64,576]{1,2,0:T(8,128)(2,1)S(1)}, u32[]{:S(2)}) copy-start(bf16[2,64,576]{1,2,0:T(8,128)(2,1)S(1)} %collective-permute-done.6) | copy-start | bytes 442372
  73.4 7.4 %collective-permute-start.7 = (bf16[2,64,576]{1,2,0:T(8,128)(2,1)S(1)}, bf16[2,64,576]{1,2,0:T(8,128)(2,1)S(1)}, u32[]{:S(2)}, u32[]{:S(2)}) collective-permute-start(bf16[2,64,576]{1,2,0:T(8,128)(2,1)S(1)} %collective-permute-done.6), channel_id=1, source_target_pairs={{0,32},{32,64},{64,96},{96,128},{128,160},{160,192},{192,224},{224... | collective-permute-start | bytes 442376 | tf_op jit(solution)/shard_map/ppermute | solution.py:18
  80.8 44.3 %copy-start.13 = (bf16[2,64,576]{1,2,0:T(8,128)(2,1)}, bf16[2,64,576]{1,2,0:T(8,128)(2,1)S(1)}, u32[]{:S(2)}) copy-start(bf16[2,64,576]{1,2,0:T(8,128)(2,1)S(1)} %collective-permute-done.7) | copy-start | bytes 442372
  80.8 7.4 %collective-permute-start.8 = (bf16[2,64,576]{1,2,0:T(8,128)(2,1)S(1)}, bf16[2,64,576]{1,2,0:T(8,128)(2,1)S(1)}, u32[]{:S(2)}, u32[]{:S(2)}) collective-permute-start(bf16[2,64,576]{1,2,0:T(8,128)(2,1)S(1)} %collective-permute-done.7), channel_id=1, source_target_pairs={{0,32},{32,64},{64,96},{96,128},{128,160},{160,192},{192,224},{224... | collective-permute-start | bytes 442376 | tf_op jit(solution)/shard_map/ppermute | solution.py:18
  88.1 36.9 %copy-start.14 = (bf16[2,64,576]{1,2,0:T(8,128)(2,1)}, bf16[2,64,576]{1,2,0:T(8,128)(2,1)S(1)}, u32[]{:S(2)}) copy-start(bf16[2,64,576]{1,2,0:T(8,128)(2,1)S(1)} %collective-permute-done.8) | copy-start | bytes 442372
  88.1 7.4 %collective-permute-start.9 = (bf16[2,64,576]{1,2,0:T(8,128)(2,1)S(1)}, bf16[2,64,576]{1,2,0:T(8,128)(2,1)S(1)}, u32[]{:S(2)}, u32[]{:S(2)}) collective-permute-start(bf16[2,64,576]{1,2,0:T(8,128)(2,1)S(1)} %collective-permute-done.8), channel_id=1, source_target_pairs={{0,32},{32,64},{64,96},{96,128},{128,160},{160,192},{192,224},{224... | collective-permute-start | bytes 442376 | tf_op jit(solution)/shard_map/ppermute | solution.py:18
  95.5 29.6 %copy-start.15 = (bf16[2,64,576]{1,2,0:T(8,128)(2,1)}, bf16[2,64,576]{1,2,0:T(8,128)(2,1)S(1)}, u32[]{:S(2)}) copy-start(bf16[2,64,576]{1,2,0:T(8,128)(2,1)S(1)} %collective-permute-done.9) | copy-start | bytes 442372
  95.5 7.4 %collective-permute-start.10 = (bf16[2,64,576]{1,2,0:T(8,128)(2,1)S(1)}, bf16[2,64,576]{1,2,0:T(8,128)(2,1)S(1)}, u32[]{:S(2)}, u32[]{:S(2)}) collective-permute-start(bf16[2,64,576]{1,2,0:T(8,128)(2,1)S(1)} %collective-permute-done.9), channel_id=1, source_target_pairs={{0,32},{32,64},{64,96},{96,128},{128,160},{160,192},{192,224},{224... | collective-permute-start | bytes 442376 | tf_op jit(solution)/shard_map/ppermute | solution.py:18
  102.8 22.2 %copy-start.16 = (bf16[2,64,576]{1,2,0:T(8,128)(2,1)}, bf16[2,64,576]{1,2,0:T(8,128)(2,1)S(1)}, u32[]{:S(2)}) copy-start(bf16[2,64,576]{1,2,0:T(8,128)(2,1)S(1)} %collective-permute-done.10) | copy-start | bytes 442372
  102.8 7.4 %collective-permute-start.11 = (bf16[2,64,576]{1,2,0:T(8,128)(2,1)S(1)}, bf16[2,64,576]{1,2,0:T(8,128)(2,1)S(1)}, u32[]{:S(2)}, u32[]{:S(2)}) collective-permute-start(bf16[2,64,576]{1,2,0:T(8,128)(2,1)S(1)} %collective-permute-done.10), channel_id=1, source_target_pairs={{0,32},{32,64},{64,96},{96,128},{128,160},{160,192},{192,224},{224... | collective-permute-start | bytes 442376 | tf_op jit(solution)/shard_map/ppermute | solution.py:18
  110.2 14.9 %copy-start.17 = (bf16[2,64,576]{1,2,0:T(8,128)(2,1)}, bf16[2,64,576]{1,2,0:T(8,128)(2,1)S(1)}, u32[]{:S(2)}) copy-start(bf16[2,64,576]{1,2,0:T(8,128)(2,1)S(1)} %collective-permute-done.11) | copy-start | bytes 442372
  110.2 7.4 %collective-permute-start.12 = (bf16[2,64,576]{1,2,0:T(8,128)(2,1)S(1)}, bf16[2,64,576]{1,2,0:T(8,128)(2,1)S(1)}, u32[]{:S(2)}, u32[]{:S(2)}) collective-permute-start(bf16[2,64,576]{1,2,0:T(8,128)(2,1)S(1)} %collective-permute-done.11), channel_id=1, source_target_pairs={{0,32},{32,64},{64,96},{96,128},{128,160},{160,192},{192,224},{224... | collective-permute-start | bytes 442376 | tf_op jit(solution)/shard_map/ppermute | solution.py:18
  117.6 7.5 %copy-start.18 = (bf16[2,64,576]{1,2,0:T(8,128)(2,1)}, bf16[2,64,576]{1,2,0:T(8,128)(2,1)S(1)}, u32[]{:S(2)}) copy-start(bf16[2,64,576]{1,2,0:T(8,128)(2,1)S(1)} %collective-permute-done.12) | copy-start | bytes 442372
  117.6 7.5 %collective-permute-start.13 = (bf16[2,64,576]{1,2,0:T(8,128)(2,1)S(1)}, bf16[2,64,576]{1,2,0:T(8,128)(2,1)}, u32[]{:S(2)}, u32[]{:S(2)}) collective-permute-start(bf16[2,64,576]{1,2,0:T(8,128)(2,1)S(1)} %collective-permute-done.12), channel_id=1, source_target_pairs={{0,32},{32,64},{64,96},{96,128},{128,160},{160,192},{192,224},{224... | collective-permute-start | bytes 442376 | tf_op jit(solution)/shard_map/ppermute | solution.py:18
  125.0 7.7 %collective-permute-start.14 = (bf16[2,64,576]{1,2,0:T(8,128)(2,1)}, bf16[2,64,576]{1,2,0:T(8,128)(2,1)}, u32[]{:S(2)}, u32[]{:S(2)}) collective-permute-start(bf16[2,64,576]{1,2,0:T(8,128)(2,1)} %collective-permute-done.13), channel_id=1, source_target_pairs={{0,32},{32,64},{64,96},{96,128},{128,160},{160,192},{192,224},{224... | collective-permute-start | bytes 442376 | tf_op jit(solution)/shard_map/ppermute | solution.py:18
  166.7 6.0 %copy-start.2 = (f32[64,8,2,1024]{3,1,2,0:T(8,128)S(1)}, f32[64,8,2,1024]{3,1,2,0:T(8,128)}, u32[]{:S(2)}) copy-start(f32[64,8,2,1024]{3,1,2,0:T(8,128)} %copy-done.1) | copy-start | bytes 12582916 | tf_op jit(solution)/shard_map/cond
  183.3 46.6 %all-to-all-start = ((bf16[32,16,2048]{2,1,0:T(8,128)(2,1)}), bf16[32,16,2048]{2,1,0:T(8,128)(2,1)S(1)}, u32[]{:S(2)}, u32[]{:S(2)}) async-start(bf16[32,16,2048]{2,1,0:T(8,128)(2,1)} %bitcast.20), calls=%async_computation | async-start | bytes 4194304 | tf_op jit(solution)/shard_map/all_to_all | solution.py:166
  245.7 10.0 %copy-start.23 = (s32[1,64,6]{1,0,2:T(1,128)S(1)}, s32[1,64,6]{1,0,2:T(1,128)}, u32[]{:S(2)}) copy-start(s32[1,64,6]{1,0,2:T(1,128)} %param.25) | copy-start | bytes 4612
  245.7 10.3 %copy-start.21 = (bf16[2048,32]{0,1:T(8,128)(2,1)S(1)}, bf16[2048,32]{0,1:T(8,128)(2,1)}, u32[]{:S(2)}) copy-start(bf16[2048,32]{0,1:T(8,128)(2,1)} %param.24) | copy-start | bytes 393220
  245.7 60.4 %all-to-all-start.1 = ((bf16[32,16,2048]{2,1,0:T(8,128)(2,1)}), bf16[32,16,2048]{2,1,0:T(8,128)(2,1)S(1)}, u32[]{:S(2)}, u32[]{:S(2)}) async-start(bf16[32,16,2048]{2,1,0:T(8,128)(2,1)} %bitcast.102), calls=%async_computation.1 | async-start | bytes 4194304 | tf_op jit(solution)/shard_map/all_to_all | solution.py:180
  (12 other events, 22.4 us)
Sparse Core Ops, SparseCore 0:
  9.5 46.7 all-gather.4
  59.5 84.4 all-gather.6
  146.1 46.5 all-gather.8
  194.5 45.1 all-gather.10
